TPU v7x, 32 devices: a whole 2x2x4 slice. The times are simulated.
32 devices in a mesh: cell: 16 (over z, y, core), bin: 2 (over x).
Axes of the slice: x: 2, y: 2, z: 4, core: 2. Of those that a mesh axis runs over, the one named last changes fastest.
Arguments:
- tensor: float32 [96, 4096, 1024], P('cell', None, 'bin'), may hold values from -6 to 6
- cell_factor: float32 [4096, 128], P('cell'), may hold values from -4 to 4
- bin_factor: float32 [1024, 128], P('bin'), may hold values from -4 to 4
Outputs:
- updated: float32 [96, 128], P('cell', 'bin')
All inputs are finite; a program needn't handle non-finite values.
Results may differ from a plain program's by a relative error of at most 0.000096.
Values sent between devices are 32-bit elements; how exact they have to be, the bound alone decides.
No kernel may reach another device: no remote copies, remote signals or barrier semaphores. Data moves between devices by JAX's collectives and lax.ppermute only.
A program may use at most 128 MiB of HBM per device.

v0:
```python
import jax
import jax.numpy as jnp
from jax import lax
from jax.sharding import PartitionSpec as P


def body(tensor, cell_factor, bin_factor):
    highest = lax.Precision.HIGHEST
    image_rows, cell_count, bin_count = tensor.shape
    rank_cols = bin_factor.shape[1]
    projected = jnp.dot(
        tensor.reshape(image_rows * cell_count, bin_count), bin_factor, precision=highest
    )
    projected = projected.reshape(image_rows, cell_count, rank_cols)
    bin_local = jnp.dot(bin_factor.T, bin_factor, precision=highest)
    gram_bin = lax.psum(bin_local, "bin")
    mttkrp = jnp.sum(
        projected * lax.all_gather(cell_factor, "cell", axis=0, tiled=True)[None, :, :], axis=1
    )
    cell_local = jnp.dot(cell_factor.T, cell_factor, precision=highest)
    gram_cell = lax.psum(cell_local, "cell")
    gram = gram_cell * gram_bin
    chol_lower = jnp.linalg.cholesky(gram)
    totals = lax.psum(mttkrp, "bin")
    solved = jax.scipy.linalg.cho_solve((chol_lower, True), totals.T).T
    own_cols = rank_cols // lax.axis_size("bin")
    updated = lax.dynamic_slice_in_dim(solved, lax.axis_index("bin") * own_cols, own_cols, 1)
    return updated


def solution(mesh):
    placed = (P("cell", None, "bin"), P("cell", None), P("bin", None))
    return jax.shard_map(
        body, mesh=mesh, in_specs=placed, out_specs=P("cell", "bin"), check_vma=False
    )
```

profile of v0, /device:TPU:0, one launch (start us, length us, event | category | flops | bytes accessed | tf_op | source)
XLA Modules:
  0.0 223.3 jit_solution(393272512199881900)
XLA Ops:
  6.5 0.0 copy-start
  6.5 0.0 all-reduce.3.cloned.1.call-start
  6.5 2.0 fusion.7
  8.6 0.0 all-reduce.3.cloned.1.call-update
  8.6 0.0 all-reduce.5.cloned.1.call-start
  8.6 0.0 copy-done
  8.6 1.2 fusion.8
  9.8 0.0 all-reduce.5.cloned.1.call-update
  9.9 0.0 all-gather.2.cloned.1.call-start
  9.9 0.7 all-gather.2.cloned.1.call-update
  10.6 87.4 %all-reduce.3.cloned.1.call-done = f32[128,128]{0,1:T(8,128)} async-done(((f32[128,128]{0,1:T(8,128)}), f32[128,128]{0,1:T(8,128)}) %all-reduce.3.cloned.1.call-update) | async-done | bytes 65552 | tf_op jit(solution)/shard_map/psum | solution.py:21
  98.0 24.7 %all-reduce.5.cloned.1.call-done = f32[128,128]{0,1:T(8,128)} async-done(((f32[128,128]{0,1:T(8,128)}), f32[128,128]{0,1:T(8,128)}) %all-reduce.5.cloned.1.call-update) | async-done | bytes 65552 | tf_op jit(solution)/shard_map/psum | solution.py:16
  122.7 0.9 mul.14
  123.6 0.1 copy.9
  123.7 11.7 %cholesky.16 = f32[128,128]{1,0:T(8,128)S(1)} custom-call(f32[128,128]{1,0:T(8,128)S(1)} %fusion.6), custom_call_target="Cholesky" | custom-call | tf_op jit(solution)/shard_map/jit(cholesky)/cholesky | solution.py:23
  135.5 0.6 compare_reduce_fusion
  136.1 0.7 fusion.1
  136.8 9.8 %custom-call.10 = f32[1,128,128]{1,2,0:T(8,128)S(1)} custom-call(f32[1,128,128]{2,1,0:T(8,128)S(1)} %fusion.1), custom_call_target="InvertDiagBlocksLowerTriangular" | custom-call | tf_op jit(solution)/shard_map/jit(_cho_solve)/triangular_solve | solution.py:25
  146.6 20.2 %all-gather.2.cloned.1.call-done = f32[4096,128]{1,0:T(8,128)} async-done(((f32[256,128]{1,0:T(8,128)}), f32[4096,128]{1,0:T(8,128)}) %all-gather.2.cloned.1.call-update) | async-done | bytes 2097168 | tf_op jit(solution)/shard_map/all_gather | solution.py:18
  166.8 43.8 %multiply_reduce_fusion = f32[6,128]{1,0:T(8,128)S(1)} fusion(f32[6,4096,512]{2,1,0:T(8,128)} %param.3, f32[4096,128]{1,0:T(8,128)} %all-gather.2.cloned.1.call-done, f32[512,128]{1,0:T(8,128)S(1)} %copy-done), kind=kOutput, calls=%fused_computation | convolution fusion | flops 19333644288 | bytes 52694016 | tf_op jit(solution)/shard_map/dot_general | solution.py:11
  210.7 4.9 %psum.23 = f32[6,128]{1,0:T(8,128)S(1)} all-reduce(f32[6,128]{1,0:T(8,128)S(1)} %multiply_reduce_fusion), channel_id=1, replica_groups=mesh['cell'=16,'bin'=2] {'bin'}, use_global_device_ids=true, to_apply=%region_5.6 | all-reduce | flops 768 | bytes 6144 | tf_op jit(solution)/shard_map/psum | solution.py:24
  215.6 0.3 fusion.4
  215.9 0.2 fusion.2
  216.1 0.7 constant_dynamic-slice_fusion
  (2 shorter events, 0.0 us)
Async XLA Ops:
  6.5 2.1 copy-start
  6.5 91.5 %all-reduce.3.cloned.1.call-start = ((), (), s32[]{:S(2)}) async-start(), calls=%async_computation | async-start | bytes 131072 | tf_op jit(solution)/shard_map/psum | solution.py:21
  8.6 114.1 %all-reduce.5.cloned.1.call-start = ((), (), s32[]{:S(2)}) async-start(), calls=%async_computation.1 | async-start | bytes 131072 | tf_op jit(solution)/shard_map/psum | solution.py:16
  9.9 156.9 %all-gather.2.cloned.1.call-start = ((), (), s32[]{:S(2)}) async-start(), calls=%async_computation.2 | async-start | bytes 2228224 | tf_op jit(solution)/shard_map/all_gather | solution.py:18
Sparse Core Ops, SparseCore 0:
  10.8 87.1 all-reduce.2
  100.3 22.3 all-reduce.4
  125.1 41.6 all-gather.1
where the time goes:
time: 224 us; the launch traced here: 223 us
  waiting for transfers between devices  133 us (59%)
  matrix products  47.5 us (21%)
  other arithmetic  23.8 us (11%)
  between operations  13.2 us (6%)
  blocking collectives  4.95 us (2%)
    psum x1, waiting for transfers between devices, body(): gram_cell = lax.psum(cell_local, 'cell')  87.4 us
    dot_general x1, matrix products, body(): jnp.dot(tensor.reshape(image_rows * cell_count, bin_count), bin_factor, p...  43.8 us
    psum x1, waiting for transfers between devices, body(): gram_bin = lax.psum(bin_local, 'bin')  24.7 us
    all_gather x1, waiting for transfers between devices, body(): lax.all_gather(cell_factor, 'cell', axis=0, tiled=True)[None, :, :]  20.2 us
    another operation x3, other arithmetic, body(): chol_lower = jnp.linalg.cholesky(gram)  12.4 us
    another operation x2, other arithmetic, body(): solved = jax.scipy.linalg.cho_solve((chol_lower, True), totals.T).T  10.5 us
    psum x1, blocking collectives, body(): totals = lax.psum(mttkrp, 'bin')  4.95 us
  transfers between devices with their start and end apart: 3, of which 3 were waited for; matrix products, arithmetic and copies ran while one was open for 11% of the time, Pallas kernels for 0%

commit v1 on v0

--- a/solution.py
+++ b/solution.py
@@ -13,7 +13,7 @@
     )
     projected = projected.reshape(image_rows, cell_count, rank_cols)
     bin_local = jnp.dot(bin_factor.T, bin_factor, precision=highest)
-    gram_bin = lax.psum(bin_local, "bin")
+    gram_bin = jnp.sum(lax.all_gather(bin_local, "bin"), axis=0)
     mttkrp = jnp.sum(
         projected * lax.all_gather(cell_factor, "cell", axis=0, tiled=True)[None, :, :], axis=1
     )

time: 224 us -> 200 us (0.89)
  waiting for transfers between devices: 133 us -> 105 us
  blocking collectives: 4.95 us -> 10.8 us
    psum x1 -> x0, waiting for transfers between devices: 24.7 us -> none  [body(): gram_bin = lax.psum(bin_local, 'bin')]
    all_gather x0 -> x1, blocking collectives: none -> 5.84 us  [body(): gram_bin = jnp.sum(lax.all_gather(bin_local, 'bin'), axis=0)]
    psum x1, waiting for transfers between devices: 87.4 us -> 82.1 us  [body(): gram_cell = lax.psum(cell_local, 'cell')]
  transfers between devices with their start and end apart: 3 -> 2, of which waited for: 3 -> 2; matrix products, arithmetic and copies ran while one was open for 11% -> 12% of each run, Pallas kernels for 0% -> 0%
where the time goes in v1:
time: 200 us
  waiting for transfers between devices  105 us (52%)
  matrix products  46.8 us (23%)
  other arithmetic  23.7 us (12%)
  between operations  13.5 us (7%)
  blocking collectives  10.8 us (5%)
    psum x1, waiting for transfers between devices, body(): gram_cell = lax.psum(cell_local, 'cell')  82.1 us
    dot_general x1, matrix products, body(): jnp.dot(tensor.reshape(image_rows * cell_count, bin_count), bin_factor, p...  43.8 us
    all_gather x1, waiting for transfers between devices, body(): lax.all_gather(cell_factor, 'cell', axis=0, tiled=True)[None, :, :]  21.7 us
    another operation x3, other arithmetic, body(): chol_lower = jnp.linalg.cholesky(gram)  12.4 us
    another operation x2, other arithmetic, body(): solved = jax.scipy.linalg.cho_solve((chol_lower, True), totals.T).T  10.5 us
    all_gather x1, blocking collectives, body(): gram_bin = jnp.sum(lax.all_gather(bin_local, 'bin'), axis=0)  5.84 us
    psum x1, blocking collectives, body(): totals = lax.psum(mttkrp, 'bin')  4.95 us
  transfers between devices with their start and end apart: 2, of which 2 were waited for; matrix products, arithmetic and copies ran while one was open for 12% of the time, Pallas kernels for 0%

profile of v1, /device:TPU:0, one launch (start us, length us, event | category | flops | bytes accessed | tf_op | source)
XLA Modules:
  0.0 200.2 jit_solution(12888665714596438592)
XLA Ops:
  6.5 0.0 copy-start
  6.5 0.0 all-reduce.2.cloned.1.call-start
  6.5 2.0 %fusion.7 = f32[128,128]{0,1:T(8,128)} fusion(f32[256,128]{1,0:T(8,128)} %param.4), kind=kOutput, calls=%fused_computation.15 | convolution fusion | flops 50331648 | bytes 196608 | tf_op jit(solution)/shard_map/dot_general | solution.py:20
  8.6 0.0 all-reduce.2.cloned.1.call-update
  8.6 0.0 all-gather.3.cloned.1.call-start
  8.6 0.7 all-gather.3.cloned.1.call-update
  9.3 0.0 copy-done
  9.3 0.6 fusion.8
  9.9 5.8 %all-gather = f32[256,128]{1,0:T(8,128)S(1)} all-gather(f32[128,128]{1,0:T(8,128)S(1)} %fusion.8), channel_id=2, replica_groups=mesh['cell'=16,'bin'=2] {'bin'}, dimensions={0}, use_global_device_ids=true | all-gather | bytes 196608 | tf_op jit(solution)/shard_map/all_gather | solution.py:16
  15.8 0.1 copy.10
  15.9 82.1 %all-reduce.2.cloned.1.call-done = f32[128,128]{0,1:T(8,128)} async-done(((f32[128,128]{0,1:T(8,128)}), f32[128,128]{0,1:T(8,128)}) %all-reduce.2.cloned.1.call-update) | async-done | bytes 65552 | tf_op jit(solution)/shard_map/psum | solution.py:21
  98.0 0.8 mul.14
  98.9 0.1 copy.11
  99.0 11.7 %cholesky.16 = f32[128,128]{1,0:T(8,128)S(1)} custom-call(f32[128,128]{1,0:T(8,128)S(1)} %fusion.6), custom_call_target="Cholesky" | custom-call | tf_op jit(solution)/shard_map/jit(cholesky)/cholesky | solution.py:23
  110.7 0.6 compare_reduce_fusion
  111.4 0.7 fusion.1
  112.0 9.8 %custom-call.10 = f32[1,128,128]{1,2,0:T(8,128)S(1)} custom-call(f32[1,128,128]{2,1,0:T(8,128)S(1)} %fusion.1), custom_call_target="InvertDiagBlocksLowerTriangular" | custom-call | tf_op jit(solution)/shard_map/jit(_cho_solve)/triangular_solve | solution.py:25
  121.8 21.7 %all-gather.3.cloned.1.call-done = f32[4096,128]{1,0:T(8,128)} async-done(((f32[256,128]{1,0:T(8,128)}), f32[4096,128]{1,0:T(8,128)}) %all-gather.3.cloned.1.call-update) | async-done | bytes 2097168 | tf_op jit(solution)/shard_map/all_gather | solution.py:18
  143.5 43.8 %multiply_reduce_fusion = f32[6,128]{1,0:T(8,128)S(1)} fusion(f32[6,4096,512]{2,1,0:T(8,128)} %param.3, f32[4096,128]{1,0:T(8,128)} %all-gather.3.cloned.1.call-done, f32[512,128]{1,0:T(8,128)S(1)} %copy-done), kind=kOutput, calls=%fused_computation | convolution fusion | flops 19333644288 | bytes 52694016 | tf_op jit(solution)/shard_map/dot_general | solution.py:11
  187.4 4.9 %psum.15 = f32[6,128]{1,0:T(8,128)S(1)} all-reduce(f32[6,128]{1,0:T(8,128)S(1)} %multiply_reduce_fusion), channel_id=1, replica_groups=mesh['cell'=16,'bin'=2] {'bin'}, use_global_device_ids=true, to_apply=%region_5.6 | all-reduce | flops 768 | bytes 6144 | tf_op jit(solution)/shard_map/psum | solution.py:24
  192.3 0.2 fusion.4
  192.5 0.2 fusion.2
  192.7 0.7 constant_dynamic-slice_fusion
  (3 shorter events, 0.1 us)
Async XLA Ops:
  6.5 2.8 %copy-start = (f32[512,128]{1,0:T(8,128)S(1)}, f32[512,128]{1,0:T(8,128)}, u32[]{:S(2)}) copy-start(f32[512,128]{1,0:T(8,128)} %param.5) | copy-start | bytes 786436
  6.5 91.5 %all-reduce.2.cloned.1.call-start = ((), (), s32[]{:S(2)}) async-start(), calls=%async_computation | async-start | bytes 131072 | tf_op jit(solution)/shard_map/psum | solution.py:21
  8.6 135.0 %all-gather.3.cloned.1.call-start = ((), (), s32[]{:S(2)}) async-start(), calls=%async_computation.1 | async-start | bytes 2228224 | tf_op jit(solution)/shard_map/all_gather | solution.py:18
Sparse Core Ops, SparseCore 0:
  10.8 87.1 all-reduce.1
  100.4 43.0 all-gather.2
